TPU v7x, 32 devices: a whole 2x2x4 slice. The times are simulated.
32 devices in a mesh: groups: 2 (over y), blk: 4 (over z), pool: 4 (over x, core).
Axes of the slice: x: 2, y: 2, z: 4, core: 2. Of those that a mesh axis runs over, the one named last changes fastest.
Arguments:
- q_new: bfloat16 [1024, 8192], P(('groups', 'blk'), 'pool'), parts along dimension 0, may hold values from -64 to 64
- kv_new: bfloat16 [1024, 8, 256], P(('groups', 'blk'), 'pool'), parts along dimension 0, may hold values from -7 to 7
- kv_cache: bfloat16 [256, 8, 128, 256], P(('groups', 'blk'), 'pool'), parts along dimension 0, may hold values from -4.5 to 4.5
- page_table: int32 [16], P('groups'), parts along dimension 0, may hold values from 0 to 127, as said below
- block_offsets: int32 [8], P('groups'), parts along dimension 0, may hold values from 0 to 3, each once
Outputs:
- attended: bfloat16 [1024, 8192], P(('groups', 'blk'), 'pool'), parts along dimension 0
There are 2 independent parts, one for each index of `groups`. A program takes and returns all parts, laid end to end along the dimension named above; each array names one. Nothing has to cross between parts.
Inputs may be any that keep to these rules, and one draw needn't show every extreme that they name: `page_table`: distinct slots; slot s lies on blk index s // 32; at most 4 entries lie on the slots of one blk index, and exactly 4 on some blk index.
All inputs are finite; a program needn't handle non-finite values.
Results may differ from a plain program's by a relative error of at most 0.0045.
Values may be sent and summed in bfloat16 or wider, within the bound.
No kernel may reach another device: no remote copies, remote signals or barrier semaphores. Data moves between devices by JAX's collectives and lax.ppermute only.
A program may use at most 64 MiB of HBM per device.

v0:
```python
import math
import jax
import jax.numpy as jnp
from jax import lax
from jax.sharding import PartitionSpec as P

PG = 2
CAP = 4


def divisor_below(total_count, upper_limit):
    for candidate in range(min(total_count, upper_limit), 0, -1):
        if total_count % candidate == 0:
            return candidate
    return 1


def attend(running, queries, entries, visible, head_size):
    maxima, totals, summed = running
    score_scale = 1.0 / math.sqrt(head_size)
    scores = (
        jnp.einsum(
            "gqd,gkd->gqk", queries, entries[..., :head_size], preferred_element_type=jnp.float32
        )
        * score_scale
    )
    scores = jnp.where(visible[None], scores, -1e30)
    row_top = jnp.maximum(maxima, jnp.max(scores, axis=2))
    factor = jnp.exp(maxima - row_top)
    weights = jnp.where(visible[None], jnp.exp(scores - row_top[..., None]), 0.0)
    totals = totals * factor + jnp.sum(weights, axis=2)
    summed = summed * factor[..., None] + jnp.einsum(
        "gqk,gkd->gqd",
        weights.astype(jnp.bfloat16),
        entries[..., head_size:],
        preferred_element_type=jnp.float32,
    )
    return (row_top, totals, summed)


def local(q_new, kv_new, kv_cache, page_table, block_offsets):
    q_rows = q_new.shape[0]
    kv_heads = kv_new.shape[1]
    head_size = kv_new.shape[2] // 2
    group_size = q_new.shape[1] // (head_size * kv_heads)
    slots_dev = kv_cache.shape[0]
    page_len = kv_cache.shape[2]
    blocks = lax.axis_size("blk")
    myself = lax.axis_index("blk")
    block_ids = jnp.arange(blocks, dtype=jnp.int32)
    my_offset = jnp.sum(jnp.where(block_ids == myself, block_offsets, 0))
    query_pos = jnp.tile(my_offset * q_rows + jnp.arange(q_rows, dtype=jnp.int32), group_size)
    queries = (
        q_new.reshape(q_rows, kv_heads, group_size, head_size)
        .transpose(1, 2, 0, 3)
        .reshape(kv_heads, group_size * q_rows, head_size)
    )
    query_span = group_size * q_rows
    running = (
        jnp.full((kv_heads, query_span), -1e30, jnp.float32),
        jnp.zeros((kv_heads, query_span), jnp.float32),
        jnp.zeros((kv_heads, query_span, head_size), jnp.float32),
    )
    carried = running
    incoming = lax.all_gather(kv_new, "blk", axis=0, tiled=True)
    row_count = incoming.shape[0]
    block_rows = divisor_below(row_count, 512)
    parted = incoming.reshape(
        row_count // block_rows, block_rows, kv_heads, 2 * head_size
    ).transpose(0, 2, 1, 3)
    row_index = jnp.arange(row_count, dtype=jnp.int32).reshape(row_count // block_rows, block_rows)

    def visit_block(state_now, block_pair):
        entries, indices = block_pair
        source = indices // q_rows
        offsets = jnp.sum(
            jnp.where(source[:, None] == block_ids[None, :], block_offsets[None, :], 0), axis=1
        )
        key_pos = offsets * q_rows + indices % q_rows
        visible = key_pos[None, :] <= query_pos[:, None]
        return (attend(state_now, queries, entries, visible, head_size), None)

    carried, unused = lax.scan(visit_block, carried, (parted, row_index))
    running = carried
    page_owner = page_table // slots_dev
    owned = page_owner == myself
    page_rank = jnp.cumsum(owned.astype(jnp.int32)) - 1
    local_slot = page_table % slots_dev
    counts = jnp.sum((page_owner[None, :] == block_ids[:, None]).astype(jnp.int32), axis=1)
    per_peer = (CAP + blocks - 1) // blocks
    starts = jnp.cumsum(counts) - counts
    my_start = jnp.sum(jnp.where(block_ids == myself, starts, 0))
    peer_slots = jnp.arange(per_peer, dtype=jnp.int32)[None, :]
    wanted = (block_ids[:, None] - my_start) % blocks + peer_slots * blocks
    picked = owned[None, None, :] & (page_rank[None, None, :] == wanted[..., None])
    chosen = jnp.sum(jnp.where(picked, local_slot[None, None, :], 0), axis=2).reshape(-1)
    received = lax.all_to_all(kv_cache[chosen], "blk", split_axis=0, concat_axis=0, tiled=True)
    arriving = (myself - starts[:, None]) % blocks + peer_slots * blocks
    present = (arriving < counts[:, None]).reshape(-1)
    order_rank = jnp.cumsum(present.astype(jnp.int32)) - 1
    choose = present[None, :] & (order_rank[None, :] == jnp.arange(PG, dtype=jnp.int32)[:, None])
    positions = jnp.sum(
        jnp.where(choose, jnp.arange(blocks * per_peer, dtype=jnp.int32)[None, :], 0), axis=1
    )
    compact = received[positions]
    valid_all = jnp.ones((blocks * PG,), jnp.bool_)
    carried = running
    incoming = lax.all_gather(compact, "blk", axis=0, tiled=True)
    page_count = incoming.shape[0]
    group_pages = divisor_below(page_count, max(1, 512 // page_len))
    parted = incoming.reshape(
        page_count // group_pages, group_pages, kv_heads, page_len, 2 * head_size
    )
    parted = parted.transpose(0, 2, 1, 3, 4).reshape(
        page_count // group_pages, kv_heads, group_pages * page_len, 2 * head_size
    )
    flags = valid_all.reshape(page_count // group_pages, group_pages)

    def visit_pages(state_now, block_pair):
        entries, present = block_pair
        visible = jnp.repeat(present, page_len)[None, :]
        return (attend(state_now, queries, entries, visible, head_size), None)

    carried, unused = lax.scan(visit_pages, carried, (parted, flags))
    running = carried
    maxima, totals, summed = running
    attended = (summed / totals[..., None]).astype(jnp.bfloat16)
    attended = attended.reshape(kv_heads, group_size, q_rows, head_size).transpose(2, 0, 1, 3)
    return attended.reshape(q_rows, kv_heads * group_size * head_size)


def solution(mesh):
    return jax.shard_map(
        local,
        mesh=mesh,
        in_specs=(
            P(("groups", "blk"), "pool"),
            P(("groups", "blk"), "pool", None),
            P(("groups", "blk"), "pool", None, None),
            P("groups"),
            P("groups"),
        ),
        out_specs=P(("groups", "blk"), "pool"),
        check_vma=False,
    )
```

profile of v0, /device:TPU:0, one launch (start us, length us, event | category | flops | bytes accessed | tf_op | source)
XLA Modules:
  0.0 93.6 jit_solution(7782781215370035208)
XLA Ops:
  6.5 0.7 and_select_fusion.3
  7.2 0.7 convert_bitcast_fusion
  8.3 1.4 %fusion.36 = (s32[]{:T(128)}, s32[]{:T(128)}) fusion(s32[4]{0:T(128)} %param.11, s32[]{:T(128)S(6)} %axis_index.15, s32[4]{0:T(128)S(1)} %convert_reduce_fusion, s32[4,1]{0,1:T(1,128)S(1)} %reduce-window.22), kind=kLoop, calls=%fused_computation.76 | loop fusion | flops 22 | bytes 60 | tf_op jit(solution)/shard_map/reduce_sum | solution.py:51
  9.7 0.7 and_select_fusion.4
  10.6 3.6 %gather_fusion = bf16[4,2,128,256]{3,2,1,0:T(8,128)(2,1)} fusion(bf16[32,2,128,256]{3,2,1,0:T(8,128)(2,1)} %param.9, s32[1024]{0:T(1024)S(1)} %pad_clamp_fusion.1), kind=kCustom, calls=%fused_computation | custom fusion | bytes 1048592 | tf_op jit(solution)/shard_map/gather | solution.py:97
  14.1 6.3 %all-to-all-start = ((bf16[4,2,128,256]{3,2,1,0:T(8,128)(2,1)}), bf16[4,2,128,256]{3,2,1,0:T(8,128)(2,1)S(1)}, u32[]{:S(2)}, u32[]{:S(2)}) async-start(bf16[4,2,128,256]{3,2,1,0:T(8,128)(2,1)} %gather_fusion), calls=%async_computation | async-start | bytes 1048576 | tf_op jit(solution)/shard_map/all_to_all | solution.py:97
  20.8 0.7 select_reduce_fusion
  21.6 0.9 copy.20
  22.5 22.8 %all_gather.6 = bf16[512,2,256]{2,0,1:T(8,128)(2,1)S(1)} all-gather(bf16[128,2,256]{2,0,1:T(8,128)(2,1)S(1)} %copy.20), channel_id=1, replica_groups=mesh['groups'=2,'blk'=4,'pool'=4] {'blk'}, dimensions={0}, use_global_device_ids=true | all-gather | bytes 655360 | tf_op jit(solution)/shard_map/all_gather | solution.py:65
  45.3 1.1 %copy.26 = bf16[16,8,16,128]{3,2,1,0:T(8,128)(2,1)S(1)} copy(bf16[16,8,16,128]{3,1,2,0:T(8,128)(2,1)} %bitcast.81) | data formatting | bytes 1048576
  47.7 1.3 %gather_fusion.1 = bf16[2,2,128,256]{3,2,1,0:T(8,128)(2,1)} fusion(bf16[4,2,128,256]{3,2,1,0:T(8,128)(2,1)S(1)} %all-to-all-done, s32[1024]{0:T(1024)S(1)} %pad_clamp_fusion), kind=kCustom, calls=%fused_computation.1 | custom fusion | bytes 524296 | tf_op jit(solution)/shard_map/gather | solution.py:105
  48.9 1.0 %fusion.14 = (f32[2,1024]{1,0:T(2,128)S(1)}, f32[2,1024,512]{1,2,0:T(8,128)S(1)}) fusion(pred[1024,512]{0,1:T(8,128)(4,1)S(1)} %broadcast_compare_fusion, bf16[2,1024,128]{2,1,0:T(8,128)(2,1)S(1)} %bitcast.72, bf16[2,512,256]{2,1,0:T(8,128)(2,1)S(1)} %bitcast.79), kind=kOutput, calls=%fused_computation.20 | convolution fusion | flops 271579136 | bytes 5513216 | tf_op jit(solution)/shard_map/while/body/eval_jaxpr/gqd,gkd->gqk/dot_general | solution.py:22
  49.9 1.1 %fusion.16 = f32[2,1024]{1,0:T(2,128)S(1)} fusion(f32[2,1024,512]{1,2,0:T(8,128)S(1)} %get-tuple-element.92, f32[2,1024]{1,0:T(2,128)S(1)} %broadcast_maximum_fusion, pred[1024,512]{0,1:T(8,128)(4,1)S(1)} %broadcast_compare_fusion), kind=kLoop, calls=%fused_computation.22 | loop fusion | flops 5240832 | bytes 4734976 | tf_op jit(solution)/shard_map/while/body/eval_jaxpr/reduce_sum | solution.py:31
  51.1 1.8 %fusion.20 = f32[2,1024,128]{2,1,0:T(8,128)S(1)} fusion(f32[2,1024,512]{1,2,0:T(8,128)S(1)} %get-tuple-element.92, f32[2,1024]{1,0:T(2,128)S(1)} %broadcast_maximum_fusion, pred[1024,512]{0,1:T(8,128)(4,1)S(1)} %broadcast_compare_fusion, f32[2,1024]{1,0:T(2,128)S(1)} %get-tuple-element.89, bf16[2,512,256]{2,1,0:T(8,128)(2,1)S(1)} %bitcast.80), kind=kOutput, calls=%fused_computation.25 | convolution fusion | flops 273940480 | bytes 6045696 | tf_op jit(solution)/shard_map/while/body/eval_jaxpr/gqk,gkd->gqd/dot_general | solution.py:32
  52.9 25.0 %all-gather.3.cloned.1.call-done = bf16[8,2,128,256]{3,2,1,0:T(8,128)(2,1)} async-done(((bf16[2,2,128,256]{3,2,1,0:T(8,128)(2,1)}), bf16[8,2,128,256]{3,2,1,0:T(8,128)(2,1)}) %all-gather.3.cloned.1.call-update) | async-done | bytes 1048592 | tf_op jit(solution)/shard_map/all_gather | solution.py:108
  77.9 1.3 %copy.22 = bf16[2,2,4,128,256]{4,3,2,1,0:T(8,128)(2,1)S(1)} copy(bf16[2,2,4,128,256]{4,3,1,2,0:T(8,128)(2,1)} %bitcast.78) | data formatting | bytes 2097152 | tf_op jit(solution)/shard_map/transpose | solution.py:114
  79.2 5.9 %while.2 = (s32[]{:T(128)}, f32[2,1024]{1,0:T(2,128)S(1)}, f32[2,1024]{1,0:T(2,128)S(1)}, f32[2,1024,128]{2,1,0:T(8,128)S(1)}, bf16[2,2,512,256]{3,2,1,0:T(8,128...) while((s32[]{:T(128)}, f32[2,1024]{1,0:T(2,128)S(1)}, f32[2,1024]{1,0:T(2,128)S(1)}, ...), condition=%wide.region_14.15_spmd, body=%wide.region_11.14_spmd.sunk | while | flops 545787904 | bytes 16908376 | solution.py:124
  79.2 0.7 bitcast_reduce_fusion.2
  80.0 0.7 fusion.57
  80.7 1.4 %fusion.58 = f32[2,1024,128]{2,1,0:T(8,128)S(1)} fusion(f32[2,512,1024]{2,1,0:T(8,128)S(1)} %get-tuple-element.137, f32[2,1024]{1,0:T(2,128)S(1)} %max.21, f32[2,1024,128]{2,1,0:T(8,128)S(1)} %get-tuple-element.150, f32[2,1024]{1,0:T(2,128)S(1)} %get-tuple-element.139, bf16[2,512,256]{2,1,0:T(8,128)(2,1)S(1)} %dynamic-slice_bitcast_fusion.2), kind=kOutput, calls=%fused_computation.10.clone.1 | convolution fusion | flops 272105472 | bytes 6569984 | tf_op jit(solution)/shard_map/while/body/eval_jaxpr/gqk,gkd->gqd/dot_general | solution.py:32
  82.2 0.7 bitcast_reduce_fusion.2
  82.9 0.7 fusion.57
  83.7 1.4 %fusion.58 = f32[2,1024,128]{2,1,0:T(8,128)S(1)} fusion(f32[2,512,1024]{2,1,0:T(8,128)S(1)} %get-tuple-element.137, f32[2,1024]{1,0:T(2,128)S(1)} %max.21, f32[2,1024,128]{2,1,0:T(8,128)S(1)} %get-tuple-element.150, f32[2,1024]{1,0:T(2,128)S(1)} %get-tuple-element.139, bf16[2,512,256]{2,1,0:T(8,128)(2,1)S(1)} %dynamic-slice_bitcast_fusion.2), kind=kOutput, calls=%fused_computation.10.clone.1 | convolution fusion | flops 272105472 | bytes 6569984 | tf_op jit(solution)/shard_map/while/body/eval_jaxpr/gqk,gkd->gqd/dot_general | solution.py:32
  85.8 0.9 copy.29
  (35 shorter events, 2.4 us)
Async XLA Ops:
  14.1 33.5 %all-to-all-start = ((bf16[4,2,128,256]{3,2,1,0:T(8,128)(2,1)}), bf16[4,2,128,256]{3,2,1,0:T(8,128)(2,1)S(1)}, u32[]{:S(2)}, u32[]{:S(2)}) async-start(bf16[4,2,128,256]{3,2,1,0:T(8,128)(2,1)} %gather_fusion), calls=%async_computation | async-start | bytes 1048576 | tf_op jit(solution)/shard_map/all_to_all | solution.py:97
  20.5 57.4 %all-gather.3.cloned.1.call-start = ((), (), s32[]{:S(2)}) async-start(), calls=%async_computation.1 | async-start | bytes 1310720 | tf_op jit(solution)/shard_map/all_gather | solution.py:108
Sparse Core Ops, SparseCore 0:
  49.1 28.7 all-gather.2
where the time goes:
time: 93.9 us; the launch traced here: 93.6 us
  waiting for transfers between devices  25 us (27%)
  blocking collectives  22.8 us (24%)
  between operations  14.2 us (15%)
  local copies, waits for them, and re-layouts  9.7 us (10%)
  other arithmetic  8.44 us (9%)
  matrix products  7.01 us (7%)
  starting transfers between devices  6.32 us (7%)
    all_gather x1, waiting for transfers between devices, local(): incoming = lax.all_gather(compact, 'blk', axis=0, tiled=True)  25 us
    all_gather x1, blocking collectives, local(): incoming = lax.all_gather(kv_new, 'blk', axis=0, tiled=True)  22.8 us
    all_to_all x1, starting transfers between devices, local(): lax.all_to_all(kv_cache[chosen], 'blk', split_axis=0, concat_axis=0, tile...  6.32 us
    dot_general x3, matrix products, attend(): jnp.einsum('gqk,gkd->gqd', weights.astype(jnp.bfloat16), entries[..., hea...  4.59 us
    gather x1, local copies, waits for them, and re-layouts, local(): kv_cache[chosen]  3.56 us
    unnamed x3, local copies, waits for them, and re-layouts  2.99 us
    reduce_sum x3, other arithmetic, attend(): totals = totals * factor + jnp.sum(weights, axis=2)  2.52 us
    dot_general x3, matrix products, attend(): jnp.einsum('gqd,gkd->gqk', queries, entries[..., :head_size], preferred_e...  2.42 us
  transfers between devices with their start and end apart: 2, of which 1 were waited for; matrix products, arithmetic and copies ran while one was open for 8% of the time, Pallas kernels for 0%

commit v1 on v0

--- a/solution.py
+++ b/solution.py
@@ -6,6 +6,22 @@
 
 PG = 2
 CAP = 4
+
+
+def collect(x, axis, dim):
+    ways, here, lap = (lax.axis_size(axis), lax.axis_index(axis), x.shape[dim])
+    dims = [n * ways if d == dim else n for d, n in enumerate(x.shape)]
+    full = lax.dynamic_update_slice_in_dim(jnp.zeros(dims, x.dtype), x, here * lap, axis=dim)
+    going_up = going_down = x
+    for far in range(1, ways // 2 + 1):
+        going_up = lax.ppermute(going_up, axis, [(d, (d + 1) % ways) for d in range(ways)])
+        full = lax.dynamic_update_slice_in_dim(full, going_up, (here - far) % ways * lap, axis=dim)
+        if 2 * far < ways:
+            going_down = lax.ppermute(going_down, axis, [(d, (d - 1) % ways) for d in range(ways)])
+            full = lax.dynamic_update_slice_in_dim(
+                full, going_down, (here + far) % ways * lap, axis=dim
+            )
+    return full
 
 
 def divisor_below(total_count, upper_limit):
@@ -105,7 +121,7 @@
     compact = received[positions]
     valid_all = jnp.ones((blocks * PG,), jnp.bool_)
     carried = running
-    incoming = lax.all_gather(compact, "blk", axis=0, tiled=True)
+    incoming = collect(compact, "blk", 0)
     page_count = incoming.shape[0]
     group_pages = divisor_below(page_count, max(1, 512 // page_len))
     parted = incoming.reshape(

time: 93.9 us -> 72.5 us (0.77)
  waiting for transfers between devices: 25 us -> 11.2 us
  between operations: 14.2 us -> 0.94 us
  starting transfers between devices: 6.32 us -> 10.2 us
  matrix products: 7.01 us -> 8.77 us
    all_gather x1 -> x0, waiting for transfers between devices: 25 us -> none  [local(): incoming = lax.all_gather(compact, 'blk', axis=0, tiled=True)]
    ppermute x0 -> x3, waiting for transfers between devices: none -> 11.2 us  [the longest x2 8.23 us: collect(): lax.ppermute(going_up, axis, [(d, (d + 1) % ways) for d in range(ways)])]
    ppermute x0 -> x3, starting transfers between devices: none -> 3.88 us  [the longest x1 2.62 us: collect(): lax.ppermute(going_down, axis, [(d, (d - 1) % ways) for d in range(ways)])]
    unnamed x3 -> x5, local copies, waits for them, and re-layouts: 2.99 us -> 4.89 us
    dot_general x3, matrix products: 4.59 us -> 6.35 us  [attend(): jnp.einsum('gqk,gkd->gqd', weights.astype(jnp.bfloat16), entries[..., hea...]
    select_n x1, other arithmetic: 0.65 us -> 2.02 us  [local(): wanted = (block_ids[:, None] - my_start) % blocks + peer_slots * blocks]
    transpose x1, local copies, waits for them, and re-layouts: 1.31 us -> 0.09 us  [local(): parted.transpose(0, 2, 1, 3, 4)]
  transfers between devices with their start and end apart: 2 -> 4, of which waited for: 1 -> 3; matrix products, arithmetic and copies ran while one was open for 8% -> 13% of each run, Pallas kernels for 0% -> 0%
where the time goes in v1:
time: 72.5 us; the launch traced here: 72.2 us
  blocking collectives  22 us (30%)
  waiting for transfers between devices  11.2 us (15%)
  starting transfers between devices  10.2 us (14%)
  local copies, waits for them, and re-layouts  9.86 us (14%)
  other arithmetic  9.07 us (13%)
  matrix products  8.77 us (12%)
  between operations  0.94 us (1%)
    all_gather x1, blocking collectives, local(): incoming = lax.all_gather(kv_new, 'blk', axis=0, tiled=True)  22 us
    ppermute x2, waiting for transfers between devices, collect(): lax.ppermute(going_up, axis, [(d, (d + 1) % ways) for d in range(ways)])  8.23 us
    dot_general x3, matrix products, attend(): jnp.einsum('gqk,gkd->gqd', weights.astype(jnp.bfloat16), entries[..., hea...  6.35 us
    all_to_all x1, starting transfers between devices, local(): lax.all_to_all(kv_cache[chosen], 'blk', split_axis=0, concat_axis=0, tile...  6.32 us
    unnamed x5, local copies, waits for them, and re-layouts  4.89 us
    gather x1, local copies, waits for them, and re-layouts, local(): kv_cache[chosen]  3.56 us
    ppermute x1, waiting for transfers between devices, collect(): lax.ppermute(going_down, axis, [(d, (d - 1) % ways) for d in range(ways)])  2.96 us
    ppermute x1, starting transfers between devices, collect(): lax.ppermute(going_down, axis, [(d, (d - 1) % ways) for d in range(ways)])  2.62 us
  transfers between devices with their start and end apart: 4, of which 3 were waited for; matrix products, arithmetic and copies ran while one was open for 13% of the time, Pallas kernels for 0%

profile of v1, /device:TPU:0, one launch (start us, length us, event | category | flops | bytes accessed | tf_op | source)
XLA Modules:
  0.0 72.2 jit_solution(559547271092609708)
XLA Ops:
  2.5 2.0 %and_select_fusion.4 = (s32[4]{0:T(128)S(1)}, s32[]{:T(128)}) fusion(s32[]{:T(128)} %fusion.37, s32[4]{0:T(128)} %param.11, s32[]{:T(128)S(6)} %axis_index.19), kind=kLoop, calls=%fused_computation.67 | loop fusion | flops 59 | bytes 44 | tf_op jit(solution)/shard_map/jit(remainder)/select_n | solution.py:110
  4.7 3.6 %gather_fusion = bf16[4,2,128,256]{3,2,1,0:T(8,128)(2,1)} fusion(bf16[32,2,128,256]{3,2,1,0:T(8,128)(2,1)} %param.9, s32[1024]{0:T(1024)S(1)} %pad_clamp_fusion.1), kind=kCustom, calls=%fused_computation | custom fusion | bytes 1048592 | tf_op jit(solution)/shard_map/gather | solution.py:113
  8.2 6.3 %all-to-all-start = ((bf16[4,2,128,256]{3,2,1,0:T(8,128)(2,1)}), bf16[4,2,128,256]{3,2,1,0:T(8,128)(2,1)S(1)}, u32[]{:S(2)}, u32[]{:S(2)}) async-start(bf16[4,2,128,256]{3,2,1,0:T(8,128)(2,1)} %gather_fusion), calls=%async_computation | async-start | bytes 1048576 | tf_op jit(solution)/shard_map/all_to_all | solution.py:113
  15.6 0.7 %select_reduce_fusion = s32[512]{0:T(512)S(1)} fusion(s32[4]{0:T(128)} %param.11, s32[512]{0:T(512)S(1)} %add_select_fusion), kind=kLoop, calls=%fused_computation.33 | loop fusion | flops 5632 | bytes 4112 | tf_op jit(solution)/shard_map/while/body/eval_jaxpr/reduce_sum | solution.py:92
  16.4 0.9 %copy.24 = bf16[128,2,256]{2,0,1:T(8,128)(2,1)S(1)} copy(bf16[128,2,256]{2,1,0:T(2,128)(2,1)} %param.8) | data formatting | bytes 262144 | tf_op args[1]
  17.3 22.0 %all_gather.3 = bf16[512,2,256]{2,0,1:T(8,128)(2,1)S(1)} all-gather(bf16[128,2,256]{2,0,1:T(8,128)(2,1)S(1)} %copy.24), channel_id=1, replica_groups=mesh['groups'=2,'blk'=4,'pool'=4] {'blk'}, dimensions={0}, use_global_device_ids=true | all-gather | bytes 655360 | tf_op jit(solution)/shard_map/all_gather | solution.py:81
  39.3 1.1 %copy.30 = bf16[16,8,16,128]{3,2,1,0:T(8,128)(2,1)S(1)} copy(bf16[16,8,16,128]{3,1,2,0:T(8,128)(2,1)} %bitcast.81) | data formatting | bytes 1048576
  41.0 1.0 %fusion.14 = (f32[2,1024]{1,0:T(2,128)S(1)}, f32[2,1024,512]{1,2,0:T(8,128)S(1)}) fusion(pred[1024,512]{0,1:T(8,128)(4,1)S(1)} %broadcast_compare_fusion, bf16[2,1024,128]{2,1,0:T(8,128)(2,1)S(1)} %bitcast.72, bf16[2,512,256]{2,1,0:T(8,128)(2,1)S(1)} %bitcast.79), kind=kOutput, calls=%fused_computation.20 | convolution fusion | flops 271579136 | bytes 5513216 | tf_op jit(solution)/shard_map/while/body/eval_jaxpr/gqd,gkd->gqk/dot_general | solution.py:38
  42.0 1.9 %copy-done = f32[2,1024,512]{1,2,0:T(8,128)} copy-done((f32[2,1024,512]{1,2,0:T(8,128)}, f32[2,1024,512]{1,2,0:T(8,128)S(1)}, u32[]{:S(2)}) %copy-start) | copy-done | bytes 4194328
  43.9 1.1 %fusion.16 = f32[2,1024]{1,0:T(2,128)S(1)} fusion(f32[2,1024,512]{1,2,0:T(8,128)S(1)} %get-tuple-element.92, f32[2,1024]{1,0:T(2,128)S(1)} %broadcast_maximum_fusion, pred[1024,512]{0,1:T(8,128)(4,1)S(1)} %broadcast_compare_fusion), kind=kLoop, calls=%fused_computation.22 | loop fusion | flops 5240832 | bytes 4734976 | tf_op jit(solution)/shard_map/while/body/eval_jaxpr/reduce_sum | solution.py:47
  45.6 1.3 %collective-permute-start = (bf16[2,2,128,256]{3,2,1,0:T(8,128)(2,1)S(1)}, bf16[2,2,128,256]{3,2,1,0:T(8,128)(2,1)S(1)}, u32[]{:S(2)}, u32[]{:S(2)}) collective-permute-start(bf16[2,2,128,256]{3,2,1,0:T(8,128)(2,1)S(1)} %gather_fusion.1), channel_id=1, source_target_pairs={{0,4},{4,8},{8,12},{12,0},{1,5},{5,9},{9,13},{13,1},{2,6},{6,10},{... | collective-permute-start | bytes 786440 | tf_op jit(solution)/shard_map/ppermute | solution.py:17
  46.9 2.6 %collective-permute-start.1 = (bf16[2,2,128,256]{3,2,1,0:T(8,128)(2,1)S(1)}, bf16[2,2,128,256]{3,2,1,0:T(8,128)(2,1)S(1)}, u32[]{:S(2)}, u32[]{:S(2)}) collective-permute-start(bf16[2,2,128,256]{3,2,1,0:T(8,128)(2,1)S(1)} %gather_fusion.1), channel_id=1, source_target_pairs={{0,12},{4,0},{8,4},{12,8},{1,13},{5,1},{9,5},{13,9},{2,14},{6,2},{... | collective-permute-start | bytes 786440 | tf_op jit(solution)/shard_map/ppermute | solution.py:20
  49.5 3.5 %fusion.20 = f32[2,1024,128]{2,1,0:T(8,128)S(1)} fusion(f32[2,1024,512]{1,2,0:T(8,128)} %copy-done, f32[2,1024]{1,0:T(2,128)S(1)} %broadcast_maximum_fusion, pred[1024,512]{0,1:T(8,128)(4,1)S(1)} %broadcast_compare_fusion, f32[2,1024]{1,0:T(2,128)S(1)} %get-tuple-element.89, bf16[2,512,256]{2,1,0:T(8,128)(2,1)S(1)} %bitcast.80), kind=kOutput, calls=%fused_computation.25 | convolution fusion | flops 273940480 | bytes 6045696 | tf_op jit(solution)/shard_map/while/body/eval_jaxpr/gqk,gkd->gqd/dot_general | solution.py:48
  53.1 3.2 %collective-permute-done = bf16[2,2,128,256]{3,2,1,0:T(8,128)(2,1)S(1)} collective-permute-done((bf16[2,2,128,256]{3,2,1,0:T(8,128)(2,1)S(1)}, bf16[2,2,128,256]{3,2,1,0:T(8,128)(2,1)S(1)}, u32[]{:S(2)}, u32[]{:S(2)}) %collective-permute-start) | collective-permute-done | bytes 262176 | tf_op jit(solution)/shard_map/ppermute | solution.py:17
  56.5 3.0 %collective-permute-done.1 = bf16[2,2,128,256]{3,2,1,0:T(8,128)(2,1)S(1)} collective-permute-done((bf16[2,2,128,256]{3,2,1,0:T(8,128)(2,1)S(1)}, bf16[2,2,128,256]{3,2,1,0:T(8,128)(2,1)S(1)}, u32[]{:S(2)}, u32[]{:S(2)}) %collective-permute-start.1) | collective-permute-done | bytes 262176 | tf_op jit(solution)/shard_map/ppermute | solution.py:20
  59.5 5.0 %collective-permute-done.2 = bf16[2,2,128,256]{3,2,1,0:T(8,128)(2,1)S(1)} collective-permute-done((bf16[2,2,128,256]{3,2,1,0:T(8,128)(2,1)S(1)}, bf16[2,2,128,256]{3,2,1,0:T(8,128)(2,1)S(1)}, u32[]{:S(2)}, u32[]{:S(2)}) %collective-permute-start.2) | collective-permute-done | bytes 262176 | tf_op jit(solution)/shard_map/ppermute | solution.py:17
  64.6 5.9 %while.2 = (s32[]{:T(128)}, f32[2,1024]{1,0:T(2,128)S(1)}, f32[2,1024]{1,0:T(2,128)S(1)}, f32[2,1024,128]{2,1,0:T(8,128)S(1)}, bf16[2,2,512,256]{3,2,1,0:T(8,128...) while((s32[]{:T(128)}, f32[2,1024]{1,0:T(2,128)S(1)}, f32[2,1024]{1,0:T(2,128)S(1)}, ...), condition=%wide.region_14.15_spmd, body=%wide.region_11.14_spmd.sunk | while | flops 545787904 | bytes 16908376 | solution.py:140
  64.7 0.7 bitcast_reduce_fusion.2
  65.4 0.7 fusion.57
  66.2 1.4 %fusion.58 = f32[2,1024,128]{2,1,0:T(8,128)S(1)} fusion(f32[2,512,1024]{2,1,0:T(8,128)S(1)} %get-tuple-element.137, f32[2,1024]{1,0:T(2,128)S(1)} %max.21, f32[2,1024,128]{2,1,0:T(8,128)S(1)} %get-tuple-element.150, f32[2,1024]{1,0:T(2,128)S(1)} %get-tuple-element.139, bf16[2,512,256]{2,1,0:T(8,128)(2,1)S(1)} %dynamic-slice_bitcast_fusion.2), kind=kOutput, calls=%fused_computation.10.clone.1 | convolution fusion | flops 272105472 | bytes 6569984 | tf_op jit(solution)/shard_map/while/body/eval_jaxpr/gqk,gkd->gqd/dot_general | solution.py:48
  67.6 0.7 bitcast_reduce_fusion.2
  68.4 0.7 fusion.57
  69.1 1.4 %fusion.58 = f32[2,1024,128]{2,1,0:T(8,128)S(1)} fusion(f32[2,512,1024]{2,1,0:T(8,128)S(1)} %get-tuple-element.137, f32[2,1024]{1,0:T(2,128)S(1)} %max.21, f32[2,1024,128]{2,1,0:T(8,128)S(1)} %get-tuple-element.150, f32[2,1024]{1,0:T(2,128)S(1)} %get-tuple-element.139, bf16[2,512,256]{2,1,0:T(8,128)(2,1)S(1)} %dynamic-slice_bitcast_fusion.2), kind=kOutput, calls=%fused_computation.10.clone.1 | convolution fusion | flops 272105472 | bytes 6569984 | tf_op jit(solution)/shard_map/while/body/eval_jaxpr/gqk,gkd->gqd/dot_general | solution.py:48
  71.2 0.9 %copy.33 = bf16[16,8,16,128]{3,1,2,0:T(8,128)(2,1)} copy(bf16[16,8,16,128]{3,2,1,0:T(8,128)(2,1)S(1)} %bitcast.77) | data formatting | bytes 1048576
  (45 shorter events, 5.2 us)
Async XLA Ops:
  8.2 36.8 %all-to-all-start = ((bf16[4,2,128,256]{3,2,1,0:T(8,128)(2,1)}), bf16[4,2,128,256]{3,2,1,0:T(8,128)(2,1)S(1)}, u32[]{:S(2)}, u32[]{:S(2)}) async-start(bf16[4,2,128,256]{3,2,1,0:T(8,128)(2,1)} %gather_fusion), calls=%async_computation | async-start | bytes 1048576 | tf_op jit(solution)/shard_map/all_to_all | solution.py:113
  42.0 1.9 %copy-start = (f32[2,1024,512]{1,2,0:T(8,128)}, f32[2,1024,512]{1,2,0:T(8,128)S(1)}, u32[]{:S(2)}) copy-start(f32[2,1024,512]{1,2,0:T(8,128)S(1)} %get-tuple-element.92) | copy-start | bytes 12582916
  45.6 10.7 %collective-permute-start = (bf16[2,2,128,256]{3,2,1,0:T(8,128)(2,1)S(1)}, bf16[2,2,128,256]{3,2,1,0:T(8,128)(2,1)S(1)}, u32[]{:S(2)}, u32[]{:S(2)}) collective-permute-start(bf16[2,2,128,256]{3,2,1,0:T(8,128)(2,1)S(1)} %gather_fusion.1), channel_id=1, source_target_pairs={{0,4},{4,8},{8,12},{12,0},{1,5},{5,9},{9,13},{13,1},{2,6},{6,10},{... | collective-permute-start | bytes 786440 | tf_op jit(solution)/shard_map/ppermute | solution.py:17
  46.9 12.6 %collective-permute-start.1 = (bf16[2,2,128,256]{3,2,1,0:T(8,128)(2,1)S(1)}, bf16[2,2,128,256]{3,2,1,0:T(8,128)(2,1)S(1)}, u32[]{:S(2)}, u32[]{:S(2)}) collective-permute-start(bf16[2,2,128,256]{3,2,1,0:T(8,128)(2,1)S(1)} %gather_fusion.1), channel_id=1, source_target_pairs={{0,12},{4,0},{8,4},{12,8},{1,13},{5,1},{9,5},{13,9},{2,14},{6,2},{... | collective-permute-start | bytes 786440 | tf_op jit(solution)/shard_map/ppermute | solution.py:20
  56.3 8.2 %collective-permute-start.2 = (bf16[2,2,128,256]{3,2,1,0:T(8,128)(2,1)S(1)}, bf16[2,2,128,256]{3,2,1,0:T(8,128)(2,1)S(1)}, u32[]{:S(2)}, u32[]{:S(2)}) collective-permute-start(bf16[2,2,128,256]{3,2,1,0:T(8,128)(2,1)S(1)} %collective-permute-done), channel_id=1, source_target_pairs={{0,4},{4,8},{8,12},{12,0},{1,5},{5,9},{9,13},{13,1},{2,6},{6,10},{... | collective-permute-start | bytes 786440 | tf_op jit(solution)/shard_map/ppermute | solution.py:17
